TPU v7x, 128 devices: a whole 4x4x4 slice. The times are simulated.
128 devices in a mesh: slab: 32 (over x, y, core), pencil: 4 (over z).
Axes of the slice: x: 4, y: 4, z: 4, core: 2. Of those that a mesh axis runs over, the one named last changes fastest.
Arguments:
- cotangent: float32 [128, 512, 512], P('slab', 'pencil'), may hold values from -6 to 6
- seg_rows: int32 [32, 4], replicated, may hold values from 1 to 64, 128 in all within a row
- owners: int32 [32, 4], replicated, may hold values from 0 to 127
- offsets: int32 [32, 4], replicated, may hold values from 0 to 64
Outputs:
- rhs_grad: float32 [128, 512, 512], P('slab', 'pencil')
- parent_grad: float32 [128, 128, 128], P(('slab', 'pencil'))
Inputs may be any that keep to these rules, and one draw needn't show every extreme that they name: `seg_rows`: each tile's 4 row counts sum to 128; in every tile one segment has exactly 64 rows.
All inputs are finite; a program needn't handle non-finite values.
Results may differ from a plain program's by a relative error of at most 0.00002.
Values sent between devices are 32-bit elements; how exact they have to be, the bound alone decides.
No kernel may reach another device: no remote copies, remote signals or barrier semaphores. Data moves between devices by JAX's collectives and lax.ppermute only.
A program may use at most 192 MiB of HBM per device.

v0:
```python
import jax
import jax.numpy as jnp
from jax import lax
from jax.sharding import PartitionSpec as P

TILE = 128
PT_DEV = 1
omega_weight = 2.0 / 3.0


def with_halo(x, sides, width):
    for axis, dim in sides:
        peers, length = (lax.axis_size(axis), x.shape[dim])
        up = [(i, (i + 1) % peers) for i in range(peers - 1)]
        down = [(j, i) for i, j in up]
        last = lax.slice_in_dim(x, length - width, length, axis=dim)
        initial = lax.slice_in_dim(x, 0, width, axis=dim)
        before = lax.ppermute(last, axis, up)
        after = lax.ppermute(initial, axis, down)
        x = jnp.concatenate([before, x, after], axis=dim)
    return x


def neighbour_sum(padded):
    total = padded[2:, 1:-1, 1:-1] + padded[:-2, 1:-1, 1:-1]
    total = total + padded[1:-1, 2:, 1:-1] + padded[1:-1, :-2, 1:-1]
    total = total + padded[1:-1, 1:-1, 2:] + padded[1:-1, 1:-1, :-2]
    return total


def block_neighbours(field):
    padded = with_halo(field, (("slab", 0), ("pencil", 1)), 1)
    return neighbour_sum(jnp.pad(padded, ((0, 0), (0, 0), (1, 1))))


def coarse_neighbours(field):
    padded = with_halo(field, (("slab", 0), ("pencil", 1)), 1)
    return neighbour_sum(jnp.pad(padded, ((0, 0), (0, 0), (1, 1))))


def coefficient(level):
    return omega_weight * 4.0**level / 6.0


def smoothed(field, neighbours):
    return (1.0 - omega_weight) * field + omega_weight / 6.0 * neighbours


def children_sum(field):
    x_cells, y_cells, z_cells = field.shape
    blocks = field.reshape(x_cells // 2, 2, y_cells // 2, 2, z_cells // 2, 2)
    return jnp.sum(blocks, axis=(1, 3, 5))


def prolong(field):
    return jnp.repeat(jnp.repeat(jnp.repeat(field, 2, axis=0), 2, axis=1), 2, axis=2)


def source_rows(seg_rows, owners, offsets, tile_size):
    starts = jnp.cumsum(seg_rows, axis=1) - seg_rows
    position = jnp.arange(tile_size, dtype=jnp.int32)[None, None, :]
    inside = (position >= starts[:, :, None]) & (position < (starts + seg_rows)[:, :, None])
    value = owners[:, :, None] * tile_size + offsets[:, :, None] + position - starts[:, :, None]
    return jnp.sum(jnp.where(inside, value, 0), axis=1)


def tile_rows(faces, tile_size):
    face_count, y_cells, z_cells = faces.shape
    blocks = faces.reshape(
        face_count, y_cells // tile_size, tile_size, z_cells // tile_size, tile_size
    )
    return blocks.transpose(0, 1, 3, 2, 4).reshape(-1, tile_size)


def add_rows(rows_data, targets, first_row, slot_count):
    shifted = targets - first_row
    segment_ids = jnp.where((shifted >= 0) & (shifted < slot_count), shifted, slot_count)
    summed = jax.ops.segment_sum(rows_data, segment_ids, num_segments=slot_count + 1)
    return summed[:slot_count]


def shards(cotangent, seg_rows, owners, offsets):
    x_cells, y_cells, z_cells = cotangent.shape
    tile_size = TILE
    grad_fine = cotangent
    rhs_grad = jnp.zeros_like(cotangent)
    for sweep_number in range(3):
        rhs_grad = rhs_grad + coefficient(0) * grad_fine
        grad_fine = smoothed(grad_fine, block_neighbours(grad_fine))
    medium = children_sum(grad_fine)
    grad_medium = jnp.zeros_like(medium)
    for sweep_number in range(3):
        grad_medium = grad_medium + coefficient(1) * medium
        medium = smoothed(medium, block_neighbours(medium))
    coarse_cot = children_sum(medium)
    grad_coarse = coefficient(2) * coarse_cot
    for sweep_number in range(2):
        coarse_cot = smoothed(coarse_cot, coarse_neighbours(coarse_cot))
        grad_coarse = grad_coarse + coefficient(2) * coarse_cot
    back_medium = prolong(grad_coarse) * 0.125
    grad_medium = grad_medium + back_medium
    medium = medium - (6.0 * back_medium - block_neighbours(back_medium)) / 4.0
    for sweep_number in range(3):
        grad_medium = grad_medium + coefficient(1) * medium
        if sweep_number < 2:
            medium = smoothed(medium, block_neighbours(medium))
    back_fine = prolong(grad_medium) * 0.125
    rhs_grad = rhs_grad + back_fine
    grad_fine = grad_fine - (6.0 * back_fine - block_neighbours(back_fine))
    for sweep_number in range(3):
        rhs_grad = rhs_grad + coefficient(0) * grad_fine
        if sweep_number < 2:
            grad_fine = smoothed(grad_fine, block_neighbours(grad_fine))
    slab_index = lax.axis_index("slab")
    slab_count = lax.axis_size("slab")
    low_part = jnp.where(slab_index == 0, rhs_grad[0], 0.0)
    high_part = jnp.where(slab_index == slab_count - 1, rhs_grad[x_cells - 1], 0.0)
    summed_faces = lax.psum(jnp.stack([low_part, high_part]), "slab")
    all_faces = lax.all_gather(summed_faces, "pencil", axis=1, tiled=True)
    all_rows = tile_rows(all_faces, tile_size)
    targets = source_rows(seg_rows, owners, offsets, tile_size)
    first_row = lax.axis_index(("slab", "pencil")) * (PT_DEV * tile_size)
    owned = add_rows(all_rows, targets.reshape(-1), first_row, PT_DEV * tile_size)
    parent_grad = owned.reshape(PT_DEV, tile_size, tile_size)
    return (rhs_grad, parent_grad)


def solution(mesh):
    return jax.shard_map(
        shards,
        mesh=mesh,
        in_specs=(P("slab", "pencil", None), P(), P(), P()),
        out_specs=(P("slab", "pencil", None), P(("slab", "pencil"), None, None)),
        check_vma=False,
    )
```

profile of v0, /device:TPU:0, one launch (start us, length us, event | category | flops | bytes accessed | tf_op | source)
XLA Modules:
  0.0 669.0 jit_solution(12144026256965964843)
XLA Ops:
  10.1 3.0 collective-permute-start.1
  14.4 2.1 fusion.93
  19.7 1.9 copy.121
  21.6 4.6 collective-permute-start.3
  29.2 3.6 select_maximum_fusion.20
  32.8 2.7 fusion.29
  36.8 5.0 collective-permute-start.5
  43.1 2.2 fusion.92
  48.5 1.9 copy.128
  50.3 4.5 collective-permute-start.7
  58.3 3.3 select_maximum_fusion.16
  61.6 2.4 fusion.24
  65.4 8.1 %collective-permute-start.9 = (f32[1,128,512]{1,2,0:T(8,128)S(1)}, f32[1,128,512]{1,2,0:T(8,128)S(1)}, u32[]{:S(2)}, u32[]{:S(2)}) collective-permute-start(f32[1,128,512]{1,2,0:T(8,128)S(1)} %get-tuple-element.34), channel_id=1, source_target_pairs={{0,4},{4,8},{8,12},{12,16},{16,20},{20,24},{24,28},{28,32},{32,36}... | collective-permute-start | bytes 786440 | tf_op jit(solution)/shard_map/ppermute | solution.py:18
  75.5 2.1 fusion.91
  80.8 1.9 copy.134
  82.7 5.0 collective-permute-start.11
  91.0 3.3 select_maximum_fusion.12
  94.4 2.4 fusion.19
  96.8 2.6 copy.138
  99.4 69.2 %reshape.120 = f32[2,2,64,2,256,2]{5,4,3,2,1,0:T(8,128)} reshape(f32[4,128,512]{2,1,0:T(8,128)} %copy.138) | data formatting | bytes 2097152 | tf_op jit(solution)/shard_map/reshape | solution.py:51
  168.6 20.8 %reduce_sum.36 = f32[2,64,256]{2,1,0:T(8,128)S(1)} reduce(f32[2,2,64,2,256,2]{5,4,3,2,1,0:T(8,128)} %reshape.120, f32[]{:T(128)} %constant.17.clone.1), dimensions={1,3,5}, to_apply=%region_0.1 | reduce | flops 229376 | bytes 1179652 | tf_op jit(solution)/shard_map/reduce_sum | solution.py:52
  190.7 7.2 %collective-permute-start.13 = (f32[1,64,256]{2,1,0:T(8,128)S(1)}, f32[1,64,256]{2,1,0:T(8,128)S(1)}, u32[]{:S(2)}, u32[]{:S(2)}) collective-permute-start(f32[1,64,256]{2,1,0:T(8,128)S(1)} %get-tuple-element.62), channel_id=1, source_target_pairs={{0,4},{4,8},{8,12},{12,16},{16,20},{20,24},{24,28},{28,32},{32,36}... | collective-permute-start | bytes 196616 | tf_op jit(solution)/shard_map/ppermute | solution.py:18
  200.0 4.5 collective-permute-start.15
  207.5 4.9 collective-permute-start.17
  214.6 4.5 collective-permute-start.19
  222.1 5.6 collective-permute-start.21
  229.9 4.5 collective-permute-start.23
  237.4 6.3 reduce_sum.38
  243.7 2.8 reduce_sum.39
  247.8 5.6 collective-permute-start.25
  255.5 4.5 collective-permute-start.27
  262.8 5.2 collective-permute-start.29
  270.1 4.5 collective-permute-start.31
  281.7 5.8 collective-permute-start.33
  295.9 4.5 collective-permute-start.35
  310.2 5.0 collective-permute-start.37
  317.4 4.6 collective-permute-start.39
  324.9 3.8 collective-permute-start.41
  330.9 4.7 collective-permute-start.43
  344.9 6.3 collective-permute-start.45
  353.2 2.0 copy.148
  357.9 2.1 fusion.90
  363.3 2.5 copy.155
  365.7 5.1 collective-permute-start.47
  371.8 1.9 mul.278
  375.5 2.0 copy.150
  377.5 2.4 copy.154
  379.9 2.4 copy.156
  382.3 3.7 select_maximum_fusion.8
  386.4 2.4 fusion.14
  390.1 5.4 collective-permute-start.49
  397.5 2.1 fusion.89
  404.7 4.8 collective-permute-start.51
  412.8 3.7 select_maximum_fusion.4
  419.3 9.8 %collective-permute-start.53 = (f32[1,128,512]{1,2,0:T(8,128)S(1)}, f32[1,128,512]{1,2,0:T(8,128)S(1)}, u32[]{:S(2)}, u32[]{:S(2)}) collective-permute-start(f32[1,128,512]{1,2,0:T(8,128)S(1)} %get-tuple-element.30), channel_id=1, source_target_pairs={{0,4},{4,8},{8,12},{12,16},{16,20},{20,24},{24,28},{28,32},{32,36}... | collective-permute-start | bytes 786440 | tf_op jit(solution)/shard_map/ppermute | solution.py:18
  431.0 2.1 fusion.88
  438.2 4.8 collective-permute-start.55
  446.4 3.7 select_maximum_fusion
  450.6 1.9 fusion.4
  454.5 138.5 %all-reduce.16.cloned.1.call-done = f32[2,128,512]{1,2,0:T(8,128)} async-done(((f32[2,128,512]{1,2,0:T(8,128)}), f32[2,128,512]{1,2,0:T(8,128)}) %all-reduce.16.cloned.1.call-update) | async-done | bytes 524304 | tf_op jit(solution)/shard_map/psum | solution.py:118
  593.2 2.5 copy.172
  595.8 32.8 %all-gather.2.cloned.1.call-done = f32[2,512,512]{1,2,0:T(8,128)} async-done(((f32[2,128,512]{1,2,0:T(8,128)}), f32[2,512,512]{1,2,0:T(8,128)}) %all-gather.2.cloned.1.call-update) | async-done | bytes 2097168 | tf_op jit(solution)/shard_map/all_gather | solution.py:119
  628.6 1.9 reshape.121
  632.4 29.0 %scatter_custom_fusion = f32[129,128]{1,0:T(8,128)S(1)} fusion(s32[4096]{0:T(1024)S(1)} %bitcast.53, f32[4096,128]{1,0:T(8,128)} %bitcast.39, f32[]{:T(128)} %constant.17.clone.1), kind=kCustom, calls=%fused_computation.276 | custom fusion | flops 524288 | bytes 66560 | tf_op jit(solution)/shard_map/scatter-add | solution.py:78
  (262 shorter events, 136.3 us)
Async XLA Ops:
  7.2 585.8 %all-reduce.16.cloned.1.call-start = ((), (), s32[]{:S(2)}) async-start(), calls=%async_computation | async-start | bytes 1048576 | tf_op jit(solution)/shard_map/psum | solution.py:118
  8.8 4.4 collective-permute-start
  10.1 4.2 collective-permute-start.1
  18.4 7.7 %collective-permute-start.2 = (f32[6,1,512]{2,1,0:T(1,128)S(1)}, f32[6,1,512]{2,1,0:T(1,128)S(1)}, u32[]{:S(2)}, u32[]{:S(2)}) collective-permute-start(f32[6,1,512]{2,1,0:T(1,128)S(1)} %copy.119), channel_id=1, source_target_pairs={{1,0},{2,1},{3,2},{5,4},{6,5},{7,6},{9,8},{10,9},{11,10},{13,12},{... | collective-permute-start | bytes 36872 | tf_op jit(solution)/shard_map/ppermute | solution.py:19
  21.6 6.0 collective-permute-start.3
  35.5 6.4 collective-permute-start.4
  36.8 6.2 collective-permute-start.5
  43.0 15.2 %copy-start.24 = (f32[1,128,512]{1,2,0:T(8,128)}, f32[1,128,512]{1,2,0:T(8,128)S(1)}, u32[]{:S(2)}) copy-start(f32[1,128,512]{1,2,0:T(8,128)S(1)} %collective-permute-done.5) | copy-start | bytes 786436
  47.2 7.7 %collective-permute-start.6 = (f32[6,1,512]{2,1,0:T(1,128)S(1)}, f32[6,1,512]{2,1,0:T(1,128)S(1)}, u32[]{:S(2)}, u32[]{:S(2)}) collective-permute-start(f32[6,1,512]{2,1,0:T(1,128)S(1)} %copy.126), channel_id=1, source_target_pairs={{1,0},{2,1},{3,2},{5,4},{6,5},{7,6},{9,8},{10,9},{11,10},{13,12},{... | collective-permute-start | bytes 36872 | tf_op jit(solution)/shard_map/ppermute | solution.py:19
  50.3 6.2 collective-permute-start.7
  64.1 9.4 %collective-permute-start.8 = (f32[1,128,512]{1,2,0:T(8,128)S(1)}, f32[1,128,512]{1,2,0:T(8,128)S(1)}, u32[]{:S(2)}, u32[]{:S(2)}) collective-permute-start(f32[1,128,512]{1,2,0:T(8,128)S(1)} %get-tuple-element.35), channel_id=1, source_target_pairs={{4,0},{8,4},{12,8},{16,12},{20,16},{24,20},{28,24},{32,28},{36,32}... | collective-permute-start | bytes 786440 | tf_op jit(solution)/shard_map/ppermute | solution.py:19
  65.4 9.3 %collective-permute-start.9 = (f32[1,128,512]{1,2,0:T(8,128)S(1)}, f32[1,128,512]{1,2,0:T(8,128)S(1)}, u32[]{:S(2)}, u32[]{:S(2)}) collective-permute-start(f32[1,128,512]{1,2,0:T(8,128)S(1)} %get-tuple-element.34), channel_id=1, source_target_pairs={{0,4},{4,8},{8,12},{12,16},{16,20},{20,24},{24,28},{28,32},{32,36}... | collective-permute-start | bytes 786440 | tf_op jit(solution)/shard_map/ppermute | solution.py:18
  79.5 8.2 %collective-permute-start.10 = (f32[6,1,512]{2,1,0:T(1,128)S(1)}, f32[6,1,512]{2,1,0:T(1,128)S(1)}, u32[]{:S(2)}, u32[]{:S(2)}) collective-permute-start(f32[6,1,512]{2,1,0:T(1,128)S(1)} %copy.132), channel_id=1, source_target_pairs={{1,0},{2,1},{3,2},{5,4},{6,5},{7,6},{9,8},{10,9},{11,10},{13,12},{... | collective-permute-start | bytes 36872 | tf_op jit(solution)/shard_map/ppermute | solution.py:19
  82.7 6.7 %collective-permute-start.11 = (f32[6,1,512]{2,1,0:T(1,128)S(1)}, f32[6,1,512]{2,1,0:T(1,128)S(1)}, u32[]{:S(2)}, u32[]{:S(2)}) collective-permute-start(f32[6,1,512]{2,1,0:T(1,128)S(1)} %copy.134), channel_id=1, source_target_pairs={{0,1},{1,2},{2,3},{4,5},{5,6},{6,7},{8,9},{9,10},{10,11},{12,13},{... | collective-permute-start | bytes 36872 | tf_op jit(solution)/shard_map/ppermute | solution.py:18
  189.4 8.5 %collective-permute-start.12 = (f32[1,64,256]{2,1,0:T(8,128)S(1)}, f32[1,64,256]{2,1,0:T(8,128)S(1)}, u32[]{:S(2)}, u32[]{:S(2)}) collective-permute-start(f32[1,64,256]{2,1,0:T(8,128)S(1)} %get-tuple-element.63), channel_id=1, source_target_pairs={{4,0},{8,4},{12,8},{16,12},{20,16},{24,20},{28,24},{32,28},{36,32}... | collective-permute-start | bytes 196616 | tf_op jit(solution)/shard_map/ppermute | solution.py:19
  190.7 8.1 %collective-permute-start.13 = (f32[1,64,256]{2,1,0:T(8,128)S(1)}, f32[1,64,256]{2,1,0:T(8,128)S(1)}, u32[]{:S(2)}, u32[]{:S(2)}) collective-permute-start(f32[1,64,256]{2,1,0:T(8,128)S(1)} %get-tuple-element.62), channel_id=1, source_target_pairs={{0,4},{4,8},{8,12},{12,16},{16,20},{20,24},{24,28},{28,32},{32,36}... | collective-permute-start | bytes 196616 | tf_op jit(solution)/shard_map/ppermute | solution.py:18
  198.7 5.8 collective-permute-start.14
  200.0 5.9 collective-permute-start.15
  206.2 6.2 collective-permute-start.16
  207.5 5.8 collective-permute-start.17
  213.3 5.8 collective-permute-start.18
  214.6 5.9 collective-permute-start.19
  220.8 6.9 %collective-permute-start.20 = (f32[1,64,256]{2,1,0:T(8,128)S(1)}, f32[1,64,256]{2,1,0:T(8,128)S(1)}, u32[]{:S(2)}, u32[]{:S(2)}) collective-permute-start(f32[1,64,256]{2,1,0:T(8,128)S(1)} %get-tuple-element.59), channel_id=1, source_target_pairs={{4,0},{8,4},{12,8},{16,12},{20,16},{24,20},{28,24},{32,28},{36,32}... | collective-permute-start | bytes 196616 | tf_op jit(solution)/shard_map/ppermute | solution.py:19
  222.1 6.5 collective-permute-start.21
  228.6 5.8 collective-permute-start.22
  229.9 5.9 collective-permute-start.23
  246.5 6.9 %collective-permute-start.24 = (f32[1,32,128]{2,1,0:T(8,128)S(1)}, f32[1,32,128]{2,1,0:T(8,128)S(1)}, u32[]{:S(2)}, u32[]{:S(2)}) collective-permute-start(f32[1,32,128]{2,1,0:T(8,128)S(1)} %bitcast.45), channel_id=1, source_target_pairs={{4,0},{8,4},{12,8},{16,12},{20,16},{24,20},{28,24},{32,28},{36,32}... | collective-permute-start | bytes 49160 | tf_op jit(solution)/shard_map/ppermute | solution.py:19
  247.8 6.4 collective-permute-start.25
  254.2 5.8 collective-permute-start.26
  255.5 5.8 collective-permute-start.27
  261.5 6.5 collective-permute-start.28
  262.8 6.0 collective-permute-start.29
  268.8 5.8 collective-permute-start.30
  270.1 5.8 collective-permute-start.31
  280.4 8.7 %collective-permute-start.32 = (f32[1,64,256]{1,2,0:T(8,128)}, f32[1,64,256]{1,2,0:T(8,128)}, u32[]{:S(2)}, u32[]{:S(2)}) collective-permute-start(f32[1,64,256]{1,2,0:T(8,128)} %bitcast.7), channel_id=1, source_target_pairs={{4,0},{8,4},{12,8},{16,12},{20,16},{24,20},{28,24},{32,28},{36,32}... | collective-permute-start | bytes 196616 | tf_op jit(solution)/shard_map/ppermute | solution.py:19
  281.7 9.0 %collective-permute-start.33 = (f32[1,64,256]{1,2,0:T(8,128)}, f32[1,64,256]{1,2,0:T(8,128)}, u32[]{:S(2)}, u32[]{:S(2)}) collective-permute-start(f32[1,64,256]{1,2,0:T(8,128)} %bitcast.7), channel_id=1, source_target_pairs={{0,4},{4,8},{8,12},{12,16},{16,20},{20,24},{24,28},{28,32},{32,36}... | collective-permute-start | bytes 196616 | tf_op jit(solution)/shard_map/ppermute | solution.py:18
  294.6 11.8 %collective-permute-start.34 = (f32[4,1,256]{2,1,0:T(1,128)S(1)}, f32[4,1,256]{2,1,0:T(1,128)S(1)}, u32[]{:S(2)}, u32[]{:S(2)}) collective-permute-start(f32[4,1,256]{2,1,0:T(1,128)S(1)} %get-tuple-element.47), channel_id=1, source_target_pairs={{1,0},{2,1},{3,2},{5,4},{6,5},{7,6},{9,8},{10,9},{11,10},{13,12},{... | collective-permute-start | bytes 12296 | tf_op jit(solution)/shard_map/ppermute | solution.py:19
  295.9 10.5 %collective-permute-start.35 = (f32[4,1,256]{2,1,0:T(1,128)S(1)}, f32[4,1,256]{2,1,0:T(1,128)S(1)}, u32[]{:S(2)}, u32[]{:S(2)}) collective-permute-start(f32[4,1,256]{2,1,0:T(1,128)S(1)} %get-tuple-element.46), channel_id=1, source_target_pairs={{0,1},{1,2},{2,3},{4,5},{5,6},{6,7},{8,9},{9,10},{10,11},{12,13},{... | collective-permute-start | bytes 12296 | tf_op jit(solution)/shard_map/ppermute | solution.py:18
  306.4 30.6 %copy-start.32 = (f32[64,256]{1,0:T(8,128)S(1)}, f32[64,256]{1,0:T(8,128)}, u32[]{:S(2)}) copy-start(f32[64,256]{1,0:T(8,128)} %copy.140) | copy-start | bytes 196612
  308.9 6.3 collective-permute-start.36
  310.2 5.9 collective-permute-start.37
  316.1 5.8 collective-permute-start.38
  317.4 5.9 collective-permute-start.39
  323.6 5.2 collective-permute-start.40
  324.9 4.7 collective-permute-start.41
  329.6 6.0 collective-permute-start.42
  330.9 5.9 collective-permute-start.43
  340.2 15.1 %collective-permute-start.44 = (f32[1,128,512]{1,2,0:T(8,128)}, f32[1,128,512]{1,2,0:T(8,128)S(1)}, u32[]{:S(2)}, u32[]{:S(2)}) collective-permute-start(f32[1,128,512]{1,2,0:T(8,128)} %bitcast.14), channel_id=1, source_target_pairs={{4,0},{8,4},{12,8},{16,12},{20,16},{24,20},{28,24},{32,28},{36,32}... | collective-permute-start | bytes 786440 | tf_op jit(solution)/shard_map/ppermute | solution.py:19
  344.9 10.3 %collective-permute-start.45 = (f32[1,128,512]{1,2,0:T(8,128)}, f32[1,128,512]{1,2,0:T(8,128)}, u32[]{:S(2)}, u32[]{:S(2)}) collective-permute-start(f32[1,128,512]{1,2,0:T(8,128)} %bitcast.16), channel_id=1, source_target_pairs={{0,4},{4,8},{8,12},{12,16},{16,20},{20,24},{24,28},{28,32},{32,36}... | collective-permute-start | bytes 786440 | tf_op jit(solution)/shard_map/ppermute | solution.py:18
  362.0 15.5 %collective-permute-start.46 = (f32[6,1,512]{2,1,0:T(1,128)S(1)}, f32[6,1,512]{2,1,0:T(1,128)}, u32[]{:S(2)}, u32[]{:S(2)}) collective-permute-start(f32[6,1,512]{2,1,0:T(1,128)S(1)} %copy.153), channel_id=1, source_target_pairs={{1,0},{2,1},{3,2},{5,4},{6,5},{7,6},{9,8},{10,9},{11,10},{13,12},{... | collective-permute-start | bytes 36872 | tf_op jit(solution)/shard_map/ppermute | solution.py:19
  365.7 14.1 %collective-permute-start.47 = (f32[6,1,512]{2,1,0:T(1,128)}, f32[6,1,512]{2,1,0:T(1,128)}, u32[]{:S(2)}, u32[]{:S(2)}) collective-permute-start(f32[6,1,512]{2,1,0:T(1,128)} %copy.155), channel_id=1, source_target_pairs={{0,1},{1,2},{2,3},{4,5},{5,6},{6,7},{8,9},{9,10},{10,11},{12,13},{... | collective-permute-start | bytes 36872 | tf_op jit(solution)/shard_map/ppermute | solution.py:18
  388.8 6.7 %collective-permute-start.48 = (f32[1,128,512]{1,2,0:T(8,128)S(1)}, f32[1,128,512]{1,2,0:T(8,128)S(1)}, u32[]{:S(2)}, u32[]{:S(2)}) collective-permute-start(f32[1,128,512]{1,2,0:T(8,128)S(1)} %get-tuple-element.33), channel_id=1, source_target_pairs={{4,0},{8,4},{12,8},{16,12},{20,16},{24,20},{28,24},{32,28},{36,32}... | collective-permute-start | bytes 786440 | tf_op jit(solution)/shard_map/ppermute | solution.py:19
  390.1 6.5 collective-permute-start.49
  401.5 7.9 %collective-permute-start.50 = (f32[6,1,512]{2,1,0:T(1,128)S(1)}, f32[6,1,512]{2,1,0:T(1,128)S(1)}, u32[]{:S(2)}, u32[]{:S(2)}) collective-permute-start(f32[6,1,512]{2,1,0:T(1,128)S(1)} %copy.159), channel_id=1, source_target_pairs={{1,0},{2,1},{3,2},{5,4},{6,5},{7,6},{9,8},{10,9},{11,10},{13,12},{... | collective-permute-start | bytes 36872 | tf_op jit(solution)/shard_map/ppermute | solution.py:19
  404.7 6.4 collective-permute-start.51
  417.9 15.2 %copy-start.6 = (f32[4,128,512]{1,2,0:T(8,128)}, f32[4,128,512]{1,2,0:T(8,128)S(1)}, u32[]{:S(2)}) copy-start(f32[4,128,512]{1,2,0:T(8,128)S(1)} %fusion.9) | copy-start | bytes 3145732
  418.0 11.1 %collective-permute-start.52 = (f32[1,128,512]{1,2,0:T(8,128)S(1)}, f32[1,128,512]{1,2,0:T(8,128)S(1)}, u32[]{:S(2)}, u32[]{:S(2)}) collective-permute-start(f32[1,128,512]{1,2,0:T(8,128)S(1)} %get-tuple-element.31), channel_id=1, source_target_pairs={{4,0},{8,4},{12,8},{16,12},{20,16},{24,20},{28,24},{32,28},{36,32}... | collective-permute-start | bytes 786440 | tf_op jit(solution)/shard_map/ppermute | solution.py:19
  419.3 10.9 %collective-permute-start.53 = (f32[1,128,512]{1,2,0:T(8,128)S(1)}, f32[1,128,512]{1,2,0:T(8,128)S(1)}, u32[]{:S(2)}, u32[]{:S(2)}) collective-permute-start(f32[1,128,512]{1,2,0:T(8,128)S(1)} %get-tuple-element.30), channel_id=1, source_target_pairs={{0,4},{4,8},{8,12},{12,16},{16,20},{20,24},{24,28},{28,32},{32,36}... | collective-permute-start | bytes 786440 | tf_op jit(solution)/shard_map/ppermute | solution.py:18
  435.0 8.0 %collective-permute-start.54 = (f32[6,1,512]{2,1,0:T(1,128)S(1)}, f32[6,1,512]{2,1,0:T(1,128)S(1)}, u32[]{:S(2)}, u32[]{:S(2)}) collective-permute-start(f32[6,1,512]{2,1,0:T(1,128)S(1)} %copy.165), channel_id=1, source_target_pairs={{1,0},{2,1},{3,2},{5,4},{6,5},{7,6},{9,8},{10,9},{11,10},{13,12},{... | collective-permute-start | bytes 36872 | tf_op jit(solution)/shard_map/ppermute | solution.py:19
  438.2 6.5 collective-permute-start.55
  450.6 142.4 %copy-start.34 = (s32[32,4]{0,1:T(4,128)S(1)}, s32[32,4]{0,1:T(4,128)}, u32[]{:S(2)}) copy-start(s32[32,4]{0,1:T(4,128)} %param.5) | copy-start | bytes 1540
  450.6 142.5 %copy-start.35 = (s32[32,4]{0,1:T(4,128)S(1)}, s32[32,4]{0,1:T(4,128)}, u32[]{:S(2)}) copy-start(s32[32,4]{0,1:T(4,128)} %param.7) | copy-start | bytes 1540
  450.6 142.5 %copy-start.36 = (s32[32,4]{0,1:T(4,128)S(1)}, s32[32,4]{0,1:T(4,128)}, u32[]{:S(2)}) copy-start(s32[32,4]{0,1:T(4,128)} %param.6) | copy-start | bytes 1540
  454.4 174.2 %all-gather.2.cloned.1.call-start = ((), (), s32[]{:S(2)}) async-start(), calls=%async_computation.1 | async-start | bytes 2621440 | tf_op jit(solution)/shard_map/all_gather | solution.py:119
  (31 other events, 112.6 us)
Sparse Core Ops, SparseCore 0:
  454.5 138.3 all-reduce.15
  594.6 33.9 all-gather.1
where the time goes:
time: 680 us; the launch traced here: 669 us
  waiting for transfers between devices  193 us (28%)
  starting transfers between devices  182 us (27%)
  local copies, waits for them, and re-layouts  181 us (27%)
  other arithmetic  97.8 us (14%)
  between operations  15.6 us (2%)
    ppermute x28, starting transfers between devices, with_halo(): before = lax.ppermute(last, axis, up)  146 us
    psum x1, waiting for transfers between devices, shards(): summed_faces = lax.psum(jnp.stack([low_part, high_part]), 'slab')  138 us
    reshape x1, local copies, waits for them, and re-layouts, children_sum(): blocks = field.reshape(x_cells // 2, 2, y_cells // 2, 2, z_cells // 2, 2)  69.2 us
    ppermute x28, starting transfers between devices, with_halo(): after = lax.ppermute(initial, axis, down)  36.1 us
    all_gather x1, waiting for transfers between devices, shards(): all_faces = lax.all_gather(summed_faces, 'pencil', axis=1, tiled=True)  32.8 us
    scatter-add x1, other arithmetic, add_rows(): jax.ops.segment_sum(rows_data, segment_ids, num_segments=slot_count + 1)  29 us
    slice x25, local copies, waits for them, and re-layouts, with_halo(): last = lax.slice_in_dim(x, length - width, length, axis=dim)  27.3 us
    concatenate x28, other arithmetic, with_halo(): x = jnp.concatenate([before, x, after], axis=dim)  26.3 us
  transfers between devices with their start and end apart: 58, of which 22 were waited for; matrix products, arithmetic and copies ran while one was open for 7% of the time, Pallas kernels for 0%

commit v1 on v0

--- a/solution.py
+++ b/solution.py
@@ -115,7 +115,9 @@
     slab_count = lax.axis_size("slab")
     low_part = jnp.where(slab_index == 0, rhs_grad[0], 0.0)
     high_part = jnp.where(slab_index == slab_count - 1, rhs_grad[x_cells - 1], 0.0)
-    summed_faces = lax.psum(jnp.stack([low_part, high_part]), "slab")
+    load = jnp.stack([low_part, high_part])
+    newest = lax.all_gather(load, axis_name="slab")
+    summed_faces = jnp.sum(newest, axis=0)
     all_faces = lax.all_gather(summed_faces, "pencil", axis=1, tiled=True)
     all_rows = tile_rows(all_faces, tile_size)
     targets = source_rows(seg_rows, owners, offsets, tile_size)

time: 680 us -> 656 us (0.965)
  waiting for transfers between devices: 193 us -> 160 us
  other arithmetic: 97.8 us -> 105 us
    psum x1 -> x0, waiting for transfers between devices: 138 us -> none  [shards(): summed_faces = lax.psum(jnp.stack([low_part, high_part]), 'slab')]
    all_gather x0 -> x1, waiting for transfers between devices: none -> 107 us  [shards(): newest = lax.all_gather(load, axis_name='slab')]
    reduce_sum x0 -> x1, other arithmetic: none -> 7.84 us  [shards(): summed_faces = jnp.sum(newest, axis=0)]
where the time goes in v1:
time: 656 us; the launch traced here: 645 us
  starting transfers between devices  183 us (28%)
  local copies, waits for them, and re-layouts  182 us (28%)
  waiting for transfers between devices  160 us (24%)
  other arithmetic  105 us (16%)
  between operations  15.6 us (2%)
    ppermute x28, starting transfers between devices, with_halo(): before = lax.ppermute(last, axis, up)  146 us
    all_gather x1, waiting for transfers between devices, shards(): newest = lax.all_gather(load, axis_name='slab')  107 us
    reshape x1, local copies, waits for them, and re-layouts, children_sum(): blocks = field.reshape(x_cells // 2, 2, y_cells // 2, 2, z_cells // 2, 2)  69.2 us
    ppermute x28, starting transfers between devices, with_halo(): after = lax.ppermute(initial, axis, down)  36.1 us
    all_gather x1, waiting for transfers between devices, shards(): all_faces = lax.all_gather(summed_faces, 'pencil', axis=1, tiled=True)  32.3 us
    scatter-add x1, other arithmetic, add_rows(): jax.ops.segment_sum(rows_data, segment_ids, num_segments=slot_count + 1)  29 us
    slice x25, local copies, waits for them, and re-layouts, with_halo(): last = lax.slice_in_dim(x, length - width, length, axis=dim)  27.3 us
    concatenate x28, other arithmetic, with_halo(): x = jnp.concatenate([before, x, after], axis=dim)  26.3 us
  transfers between devices with their start and end apart: 58, of which 22 were waited for; matrix products, arithmetic and copies ran while one was open for 7% of the time, Pallas kernels for 0%

profile of v1, /device:TPU:0, one launch (start us, length us, event | category | flops | bytes accessed | tf_op | source)
XLA Modules:
  0.0 644.9 jit_solution(2014478268066024557)
XLA Ops:
  10.1 3.0 collective-permute-start.1
  14.4 2.1 fusion.93
  21.6 4.6 collective-permute-start.3
  29.2 3.6 select_maximum_fusion.20
  32.8 2.7 fusion.29
  36.8 5.0 collective-permute-start.5
  43.1 2.2 fusion.92
  50.3 4.5 collective-permute-start.7
  58.2 3.3 select_maximum_fusion.16
  61.6 2.4 fusion.24
  65.4 8.1 %collective-permute-start.9 = (f32[1,128,512]{1,2,0:T(8,128)S(1)}, f32[1,128,512]{1,2,0:T(8,128)S(1)}, u32[]{:S(2)}, u32[]{:S(2)}) collective-permute-start(f32[1,128,512]{1,2,0:T(8,128)S(1)} %get-tuple-element.34), channel_id=1, source_target_pairs={{0,4},{4,8},{8,12},{12,16},{16,20},{20,24},{24,28},{28,32},{32,36}... | collective-permute-start | bytes 786440 | tf_op jit(solution)/shard_map/ppermute | solution.py:18
  75.5 2.1 fusion.91
  80.8 1.9 copy.135
  82.6 5.1 collective-permute-start.11
  91.1 3.3 select_maximum_fusion.12
  94.5 2.4 fusion.19
  96.9 2.6 copy.139
  99.4 69.2 %reshape.120 = f32[2,2,64,2,256,2]{5,4,3,2,1,0:T(8,128)} reshape(f32[4,128,512]{2,1,0:T(8,128)} %copy.139) | data formatting | bytes 2097152 | tf_op jit(solution)/shard_map/reshape | solution.py:51
  168.6 20.8 %reduce_sum.45 = f32[2,64,256]{2,1,0:T(8,128)S(1)} reduce(f32[2,2,64,2,256,2]{5,4,3,2,1,0:T(8,128)} %reshape.120, f32[]{:T(128)} %constant.17.clone.1), dimensions={1,3,5}, to_apply=%region_0.1 | reduce | flops 229376 | bytes 1179652 | tf_op jit(solution)/shard_map/reduce_sum | solution.py:52
  190.7 7.2 %collective-permute-start.13 = (f32[1,64,256]{2,1,0:T(8,128)S(1)}, f32[1,64,256]{2,1,0:T(8,128)S(1)}, u32[]{:S(2)}, u32[]{:S(2)}) collective-permute-start(f32[1,64,256]{2,1,0:T(8,128)S(1)} %get-tuple-element.62), channel_id=1, source_target_pairs={{0,4},{4,8},{8,12},{12,16},{16,20},{20,24},{24,28},{28,32},{32,36}... | collective-permute-start | bytes 196616 | tf_op jit(solution)/shard_map/ppermute | solution.py:18
  200.1 4.5 collective-permute-start.15
  207.6 4.9 collective-permute-start.17
  214.6 4.5 collective-permute-start.19
  222.1 5.6 collective-permute-start.21
  229.9 4.5 collective-permute-start.23
  237.4 6.3 reduce_sum.47
  243.7 2.8 reduce_sum.48
  247.8 5.6 collective-permute-start.25
  255.5 4.5 collective-permute-start.27
  262.8 5.2 collective-permute-start.29
  270.2 4.5 collective-permute-start.31
  281.7 5.8 collective-permute-start.33
  295.9 4.5 collective-permute-start.35
  310.3 5.0 collective-permute-start.37
  317.5 4.6 collective-permute-start.39
  325.0 3.8 collective-permute-start.41
  331.0 4.7 collective-permute-start.43
  345.1 6.3 collective-permute-start.45
  353.4 2.1 copy.149
  358.1 2.1 fusion.90
  363.4 2.5 copy.156
  365.9 5.1 collective-permute-start.47
  372.0 1.9 mul.278
  375.7 2.0 copy.151
  377.7 2.4 copy.155
  380.1 2.4 copy.157
  382.5 3.7 select_maximum_fusion.8
  386.6 2.4 fusion.14
  390.3 5.4 collective-permute-start.49
  397.6 2.1 fusion.89
  403.0 1.9 copy.162
  404.8 4.8 collective-permute-start.51
  413.0 3.7 select_maximum_fusion.4
  419.5 9.8 %collective-permute-start.53 = (f32[1,128,512]{1,2,0:T(8,128)S(1)}, f32[1,128,512]{1,2,0:T(8,128)S(1)}, u32[]{:S(2)}, u32[]{:S(2)}) collective-permute-start(f32[1,128,512]{1,2,0:T(8,128)S(1)} %get-tuple-element.30), channel_id=1, source_target_pairs={{0,4},{4,8},{8,12},{12,16},{16,20},{20,24},{24,28},{28,32},{32,36}... | collective-permute-start | bytes 786440 | tf_op jit(solution)/shard_map/ppermute | solution.py:18
  431.2 2.1 fusion.88
  436.5 1.9 copy.168
  438.4 4.8 collective-permute-start.55
  446.6 3.7 select_maximum_fusion
  450.7 1.9 fusion.4
  455.0 106.6 %all-gather.6.cloned.1.call-done = f32[64,128,512]{2,1,0:T(8,128)} async-done(((f32[2,128,512]{2,1,0:T(8,128)}), f32[64,128,512]{2,1,0:T(8,128)}) %all-gather.6.cloned.1.call-update) | async-done | bytes 16777232 | tf_op jit(solution)/shard_map/all_gather | solution.py:119
  561.7 7.8 %reduce_sum.51 = f32[2,128,512]{2,1,0:T(8,128)S(1)} reduce(f32[32,2,128,512]{3,2,1,0:T(8,128)} %bitcast.39, f32[]{:T(128)} %constant.17.clone.1), dimensions={0}, to_apply=%region_5.6 | reduce | flops 4063232 | bytes 17301508 | tf_op jit(solution)/shard_map/reduce_sum | solution.py:120
  572.1 32.3 %all-gather.4.cloned.1.call-done = f32[2,512,512]{1,2,0:T(8,128)} async-done(((f32[2,128,512]{1,2,0:T(8,128)}), f32[2,512,512]{1,2,0:T(8,128)}) %all-gather.4.cloned.1.call-update) | async-done | bytes 2097168 | tf_op jit(solution)/shard_map/all_gather | solution.py:121
  604.4 1.9 reshape.133
  608.2 29.0 %scatter_custom_fusion = f32[129,128]{1,0:T(8,128)S(1)} fusion(s32[4096]{0:T(1024)S(1)} %bitcast.56, f32[4096,128]{1,0:T(8,128)} %bitcast.42, f32[]{:T(128)} %constant.17.clone.1), kind=kCustom, calls=%fused_computation.276 | custom fusion | flops 524288 | bytes 66560 | tf_op jit(solution)/shard_map/scatter-add | solution.py:78
  (267 shorter events, 139.1 us)
Async XLA Ops:
  7.2 554.5 %all-gather.6.cloned.1.call-start = ((), (), s32[]{:S(2)}) async-start(), calls=%async_computation.1 | async-start | bytes 17301504 | tf_op jit(solution)/shard_map/all_gather | solution.py:119
  8.8 4.4 collective-permute-start
  10.1 4.2 collective-permute-start.1
  18.4 7.7 %collective-permute-start.2 = (f32[6,1,512]{2,1,0:T(1,128)S(1)}, f32[6,1,512]{2,1,0:T(1,128)S(1)}, u32[]{:S(2)}, u32[]{:S(2)}) collective-permute-start(f32[6,1,512]{2,1,0:T(1,128)S(1)} %copy.120), channel_id=1, source_target_pairs={{1,0},{2,1},{3,2},{5,4},{6,5},{7,6},{9,8},{10,9},{11,10},{13,12},{... | collective-permute-start | bytes 36872 | tf_op jit(solution)/shard_map/ppermute | solution.py:19
  21.6 6.0 collective-permute-start.3
  35.5 6.4 collective-permute-start.4
  36.8 6.2 collective-permute-start.5
  43.0 15.2 %copy-start.25 = (f32[1,128,512]{1,2,0:T(8,128)}, f32[1,128,512]{1,2,0:T(8,128)S(1)}, u32[]{:S(2)}) copy-start(f32[1,128,512]{1,2,0:T(8,128)S(1)} %collective-permute-done.5) | copy-start | bytes 786436
  47.2 7.7 %collective-permute-start.6 = (f32[6,1,512]{2,1,0:T(1,128)S(1)}, f32[6,1,512]{2,1,0:T(1,128)S(1)}, u32[]{:S(2)}, u32[]{:S(2)}) collective-permute-start(f32[6,1,512]{2,1,0:T(1,128)S(1)} %copy.127), channel_id=1, source_target_pairs={{1,0},{2,1},{3,2},{5,4},{6,5},{7,6},{9,8},{10,9},{11,10},{13,12},{... | collective-permute-start | bytes 36872 | tf_op jit(solution)/shard_map/ppermute | solution.py:19
  50.3 6.2 collective-permute-start.7
  64.1 9.4 %collective-permute-start.8 = (f32[1,128,512]{1,2,0:T(8,128)S(1)}, f32[1,128,512]{1,2,0:T(8,128)S(1)}, u32[]{:S(2)}, u32[]{:S(2)}) collective-permute-start(f32[1,128,512]{1,2,0:T(8,128)S(1)} %get-tuple-element.35), channel_id=1, source_target_pairs={{4,0},{8,4},{12,8},{16,12},{20,16},{24,20},{28,24},{32,28},{36,32}... | collective-permute-start | bytes 786440 | tf_op jit(solution)/shard_map/ppermute | solution.py:19
  65.4 9.3 %collective-permute-start.9 = (f32[1,128,512]{1,2,0:T(8,128)S(1)}, f32[1,128,512]{1,2,0:T(8,128)S(1)}, u32[]{:S(2)}, u32[]{:S(2)}) collective-permute-start(f32[1,128,512]{1,2,0:T(8,128)S(1)} %get-tuple-element.34), channel_id=1, source_target_pairs={{0,4},{4,8},{8,12},{12,16},{16,20},{20,24},{24,28},{28,32},{32,36}... | collective-permute-start | bytes 786440 | tf_op jit(solution)/shard_map/ppermute | solution.py:18
  79.5 8.3 %collective-permute-start.10 = (f32[6,1,512]{2,1,0:T(1,128)S(1)}, f32[6,1,512]{2,1,0:T(1,128)S(1)}, u32[]{:S(2)}, u32[]{:S(2)}) collective-permute-start(f32[6,1,512]{2,1,0:T(1,128)S(1)} %copy.133), channel_id=1, source_target_pairs={{1,0},{2,1},{3,2},{5,4},{6,5},{7,6},{9,8},{10,9},{11,10},{13,12},{... | collective-permute-start | bytes 36872 | tf_op jit(solution)/shard_map/ppermute | solution.py:19
  82.6 6.8 %collective-permute-start.11 = (f32[6,1,512]{2,1,0:T(1,128)S(1)}, f32[6,1,512]{2,1,0:T(1,128)S(1)}, u32[]{:S(2)}, u32[]{:S(2)}) collective-permute-start(f32[6,1,512]{2,1,0:T(1,128)S(1)} %copy.135), channel_id=1, source_target_pairs={{0,1},{1,2},{2,3},{4,5},{5,6},{6,7},{8,9},{9,10},{10,11},{12,13},{... | collective-permute-start | bytes 36872 | tf_op jit(solution)/shard_map/ppermute | solution.py:18
  189.4 8.5 %collective-permute-start.12 = (f32[1,64,256]{2,1,0:T(8,128)S(1)}, f32[1,64,256]{2,1,0:T(8,128)S(1)}, u32[]{:S(2)}, u32[]{:S(2)}) collective-permute-start(f32[1,64,256]{2,1,0:T(8,128)S(1)} %get-tuple-element.63), channel_id=1, source_target_pairs={{4,0},{8,4},{12,8},{16,12},{20,16},{24,20},{28,24},{32,28},{36,32}... | collective-permute-start | bytes 196616 | tf_op jit(solution)/shard_map/ppermute | solution.py:19
  190.7 8.1 %collective-permute-start.13 = (f32[1,64,256]{2,1,0:T(8,128)S(1)}, f32[1,64,256]{2,1,0:T(8,128)S(1)}, u32[]{:S(2)}, u32[]{:S(2)}) collective-permute-start(f32[1,64,256]{2,1,0:T(8,128)S(1)} %get-tuple-element.62), channel_id=1, source_target_pairs={{0,4},{4,8},{8,12},{12,16},{16,20},{20,24},{24,28},{28,32},{32,36}... | collective-permute-start | bytes 196616 | tf_op jit(solution)/shard_map/ppermute | solution.py:18
  198.8 5.8 collective-permute-start.14
  200.1 5.9 collective-permute-start.15
  206.3 6.2 collective-permute-start.16
  207.6 5.8 collective-permute-start.17
  213.3 5.8 collective-permute-start.18
  214.6 5.9 collective-permute-start.19
  220.8 6.9 %collective-permute-start.20 = (f32[1,64,256]{2,1,0:T(8,128)S(1)}, f32[1,64,256]{2,1,0:T(8,128)S(1)}, u32[]{:S(2)}, u32[]{:S(2)}) collective-permute-start(f32[1,64,256]{2,1,0:T(8,128)S(1)} %get-tuple-element.59), channel_id=1, source_target_pairs={{4,0},{8,4},{12,8},{16,12},{20,16},{24,20},{28,24},{32,28},{36,32}... | collective-permute-start | bytes 196616 | tf_op jit(solution)/shard_map/ppermute | solution.py:19
  222.1 6.5 %collective-permute-start.21 = (f32[1,64,256]{2,1,0:T(8,128)S(1)}, f32[1,64,256]{2,1,0:T(8,128)S(1)}, u32[]{:S(2)}, u32[]{:S(2)}) collective-permute-start(f32[1,64,256]{2,1,0:T(8,128)S(1)} %get-tuple-element.58), channel_id=1, source_target_pairs={{0,4},{4,8},{8,12},{12,16},{16,20},{20,24},{24,28},{28,32},{32,36}... | collective-permute-start | bytes 196616 | tf_op jit(solution)/shard_map/ppermute | solution.py:18
  228.6 5.8 collective-permute-start.22
  229.9 5.9 collective-permute-start.23
  246.5 6.9 %collective-permute-start.24 = (f32[1,32,128]{2,1,0:T(8,128)S(1)}, f32[1,32,128]{2,1,0:T(8,128)S(1)}, u32[]{:S(2)}, u32[]{:S(2)}) collective-permute-start(f32[1,32,128]{2,1,0:T(8,128)S(1)} %bitcast.48), channel_id=1, source_target_pairs={{4,0},{8,4},{12,8},{16,12},{20,16},{24,20},{28,24},{32,28},{36,32}... | collective-permute-start | bytes 49160 | tf_op jit(solution)/shard_map/ppermute | solution.py:19
  247.8 6.4 collective-permute-start.25
  254.2 5.8 collective-permute-start.26
  255.5 5.8 collective-permute-start.27
  261.6 6.5 %collective-permute-start.28 = (f32[1,32,128]{2,1,0:T(8,128)S(1)}, f32[1,32,128]{2,1,0:T(8,128)S(1)}, u32[]{:S(2)}, u32[]{:S(2)}) collective-permute-start(f32[1,32,128]{2,1,0:T(8,128)S(1)} %fusion.81), channel_id=1, source_target_pairs={{4,0},{8,4},{12,8},{16,12},{20,16},{24,20},{28,24},{32,28},{36,32}... | collective-permute-start | bytes 49160 | tf_op jit(solution)/shard_map/ppermute | solution.py:19
  262.8 6.0 collective-permute-start.29
  268.9 5.8 collective-permute-start.30
  270.2 5.8 collective-permute-start.31
  280.5 8.7 %collective-permute-start.32 = (f32[1,64,256]{1,2,0:T(8,128)}, f32[1,64,256]{1,2,0:T(8,128)}, u32[]{:S(2)}, u32[]{:S(2)}) collective-permute-start(f32[1,64,256]{1,2,0:T(8,128)} %bitcast.7), channel_id=1, source_target_pairs={{4,0},{8,4},{12,8},{16,12},{20,16},{24,20},{28,24},{32,28},{36,32}... | collective-permute-start | bytes 196616 | tf_op jit(solution)/shard_map/ppermute | solution.py:19
  281.7 9.0 %collective-permute-start.33 = (f32[1,64,256]{1,2,0:T(8,128)}, f32[1,64,256]{1,2,0:T(8,128)}, u32[]{:S(2)}, u32[]{:S(2)}) collective-permute-start(f32[1,64,256]{1,2,0:T(8,128)} %bitcast.7), channel_id=1, source_target_pairs={{0,4},{4,8},{8,12},{12,16},{16,20},{20,24},{24,28},{28,32},{32,36}... | collective-permute-start | bytes 196616 | tf_op jit(solution)/shard_map/ppermute | solution.py:18
  294.6 11.9 %collective-permute-start.34 = (f32[4,1,256]{2,1,0:T(1,128)S(1)}, f32[4,1,256]{2,1,0:T(1,128)S(1)}, u32[]{:S(2)}, u32[]{:S(2)}) collective-permute-start(f32[4,1,256]{2,1,0:T(1,128)S(1)} %get-tuple-element.47), channel_id=1, source_target_pairs={{1,0},{2,1},{3,2},{5,4},{6,5},{7,6},{9,8},{10,9},{11,10},{13,12},{... | collective-permute-start | bytes 12296 | tf_op jit(solution)/shard_map/ppermute | solution.py:19
  295.9 10.6 %collective-permute-start.35 = (f32[4,1,256]{2,1,0:T(1,128)S(1)}, f32[4,1,256]{2,1,0:T(1,128)S(1)}, u32[]{:S(2)}, u32[]{:S(2)}) collective-permute-start(f32[4,1,256]{2,1,0:T(1,128)S(1)} %get-tuple-element.46), channel_id=1, source_target_pairs={{0,1},{1,2},{2,3},{4,5},{5,6},{6,7},{8,9},{9,10},{10,11},{12,13},{... | collective-permute-start | bytes 12296 | tf_op jit(solution)/shard_map/ppermute | solution.py:18
  306.5 30.6 %copy-start.33 = (f32[64,256]{1,0:T(8,128)S(1)}, f32[64,256]{1,0:T(8,128)}, u32[]{:S(2)}) copy-start(f32[64,256]{1,0:T(8,128)} %copy.141) | copy-start | bytes 196612
  309.0 6.3 collective-permute-start.36
  310.3 5.9 collective-permute-start.37
  316.2 5.8 collective-permute-start.38
  317.5 5.9 collective-permute-start.39
  323.7 5.2 collective-permute-start.40
  325.0 4.7 collective-permute-start.41
  329.7 6.0 collective-permute-start.42
  331.0 5.9 collective-permute-start.43
  340.3 15.1 %collective-permute-start.44 = (f32[1,128,512]{1,2,0:T(8,128)}, f32[1,128,512]{1,2,0:T(8,128)S(1)}, u32[]{:S(2)}, u32[]{:S(2)}) collective-permute-start(f32[1,128,512]{1,2,0:T(8,128)} %bitcast.14), channel_id=1, source_target_pairs={{4,0},{8,4},{12,8},{16,12},{20,16},{24,20},{28,24},{32,28},{36,32}... | collective-permute-start | bytes 786440 | tf_op jit(solution)/shard_map/ppermute | solution.py:19
  345.1 10.4 %collective-permute-start.45 = (f32[1,128,512]{1,2,0:T(8,128)}, f32[1,128,512]{1,2,0:T(8,128)}, u32[]{:S(2)}, u32[]{:S(2)}) collective-permute-start(f32[1,128,512]{1,2,0:T(8,128)} %bitcast.16), channel_id=1, source_target_pairs={{0,4},{4,8},{8,12},{12,16},{16,20},{20,24},{24,28},{28,32},{32,36}... | collective-permute-start | bytes 786440 | tf_op jit(solution)/shard_map/ppermute | solution.py:18
  358.1 12.9 %copy-start.34 = (f32[2,64,256]{2,1,0:T(8,128)S(1)}, f32[2,64,256]{2,1,0:T(8,128)}, u32[]{:S(2)}) copy-start(f32[2,64,256]{2,1,0:T(8,128)} %get-tuple-element.11) | copy-start | bytes 393220
  362.1 15.6 %collective-permute-start.46 = (f32[6,1,512]{2,1,0:T(1,128)S(1)}, f32[6,1,512]{2,1,0:T(1,128)}, u32[]{:S(2)}, u32[]{:S(2)}) collective-permute-start(f32[6,1,512]{2,1,0:T(1,128)S(1)} %copy.154), channel_id=1, source_target_pairs={{1,0},{2,1},{3,2},{5,4},{6,5},{7,6},{9,8},{10,9},{11,10},{13,12},{... | collective-permute-start | bytes 36872 | tf_op jit(solution)/shard_map/ppermute | solution.py:19
  365.9 14.2 %collective-permute-start.47 = (f32[6,1,512]{2,1,0:T(1,128)}, f32[6,1,512]{2,1,0:T(1,128)}, u32[]{:S(2)}, u32[]{:S(2)}) collective-permute-start(f32[6,1,512]{2,1,0:T(1,128)} %copy.156), channel_id=1, source_target_pairs={{0,1},{1,2},{2,3},{4,5},{5,6},{6,7},{8,9},{9,10},{10,11},{12,13},{... | collective-permute-start | bytes 36872 | tf_op jit(solution)/shard_map/ppermute | solution.py:18
  388.9 10.9 %copy-start = (f32[4,128,512]{1,2,0:T(8,128)}, f32[4,128,512]{1,2,0:T(8,128)S(1)}, u32[]{:S(2)}) copy-start(f32[4,128,512]{1,2,0:T(8,128)S(1)} %fusion.14) | copy-start | bytes 3145732
  389.0 6.7 %collective-permute-start.48 = (f32[1,128,512]{1,2,0:T(8,128)S(1)}, f32[1,128,512]{1,2,0:T(8,128)S(1)}, u32[]{:S(2)}, u32[]{:S(2)}) collective-permute-start(f32[1,128,512]{1,2,0:T(8,128)S(1)} %get-tuple-element.33), channel_id=1, source_target_pairs={{4,0},{8,4},{12,8},{16,12},{20,16},{24,20},{28,24},{32,28},{36,32}... | collective-permute-start | bytes 786440 | tf_op jit(solution)/shard_map/ppermute | solution.py:19
  390.3 6.5 %collective-permute-start.49 = (f32[1,128,512]{1,2,0:T(8,128)S(1)}, f32[1,128,512]{1,2,0:T(8,128)S(1)}, u32[]{:S(2)}, u32[]{:S(2)}) collective-permute-start(f32[1,128,512]{1,2,0:T(8,128)S(1)} %get-tuple-element.32), channel_id=1, source_target_pairs={{0,4},{4,8},{8,12},{12,16},{16,20},{20,24},{24,28},{28,32},{32,36}... | collective-permute-start | bytes 786440 | tf_op jit(solution)/shard_map/ppermute | solution.py:18
  401.7 7.9 %collective-permute-start.50 = (f32[6,1,512]{2,1,0:T(1,128)S(1)}, f32[6,1,512]{2,1,0:T(1,128)S(1)}, u32[]{:S(2)}, u32[]{:S(2)}) collective-permute-start(f32[6,1,512]{2,1,0:T(1,128)S(1)} %copy.160), channel_id=1, source_target_pairs={{1,0},{2,1},{3,2},{5,4},{6,5},{7,6},{9,8},{10,9},{11,10},{13,12},{... | collective-permute-start | bytes 36872 | tf_op jit(solution)/shard_map/ppermute | solution.py:19
  404.8 6.4 collective-permute-start.51
  418.1 15.2 %copy-start.6 = (f32[4,128,512]{1,2,0:T(8,128)}, f32[4,128,512]{1,2,0:T(8,128)S(1)}, u32[]{:S(2)}) copy-start(f32[4,128,512]{1,2,0:T(8,128)S(1)} %fusion.9) | copy-start | bytes 3145732
  418.2 11.1 %collective-permute-start.52 = (f32[1,128,512]{1,2,0:T(8,128)S(1)}, f32[1,128,512]{1,2,0:T(8,128)S(1)}, u32[]{:S(2)}, u32[]{:S(2)}) collective-permute-start(f32[1,128,512]{1,2,0:T(8,128)S(1)} %get-tuple-element.31), channel_id=1, source_target_pairs={{4,0},{8,4},{12,8},{16,12},{20,16},{24,20},{28,24},{32,28},{36,32}... | collective-permute-start | bytes 786440 | tf_op jit(solution)/shard_map/ppermute | solution.py:19
  419.5 10.9 %collective-permute-start.53 = (f32[1,128,512]{1,2,0:T(8,128)S(1)}, f32[1,128,512]{1,2,0:T(8,128)S(1)}, u32[]{:S(2)}, u32[]{:S(2)}) collective-permute-start(f32[1,128,512]{1,2,0:T(8,128)S(1)} %get-tuple-element.30), channel_id=1, source_target_pairs={{0,4},{4,8},{8,12},{12,16},{16,20},{20,24},{24,28},{28,32},{32,36}... | collective-permute-start | bytes 786440 | tf_op jit(solution)/shard_map/ppermute | solution.py:18
  435.2 8.0 %collective-permute-start.54 = (f32[6,1,512]{2,1,0:T(1,128)S(1)}, f32[6,1,512]{2,1,0:T(1,128)S(1)}, u32[]{:S(2)}, u32[]{:S(2)}) collective-permute-start(f32[6,1,512]{2,1,0:T(1,128)S(1)} %copy.166), channel_id=1, source_target_pairs={{1,0},{2,1},{3,2},{5,4},{6,5},{7,6},{9,8},{10,9},{11,10},{13,12},{... | collective-permute-start | bytes 36872 | tf_op jit(solution)/shard_map/ppermute | solution.py:19
  438.4 6.5 %collective-permute-start.55 = (f32[6,1,512]{2,1,0:T(1,128)S(1)}, f32[6,1,512]{2,1,0:T(1,128)S(1)}, u32[]{:S(2)}, u32[]{:S(2)}) collective-permute-start(f32[6,1,512]{2,1,0:T(1,128)S(1)} %copy.168), channel_id=1, source_target_pairs={{0,1},{1,2},{2,3},{4,5},{5,6},{6,7},{8,9},{9,10},{10,11},{12,13},{... | collective-permute-start | bytes 36872 | tf_op jit(solution)/shard_map/ppermute | solution.py:18
  454.7 149.7 %all-gather.4.cloned.1.call-start = ((), (), s32[]{:S(2)}) async-start(), calls=%async_computation | async-start | bytes 2621440 | tf_op jit(solution)/shard_map/all_gather | solution.py:121
  561.7 9.1 %copy-start.22 = (f32[4,128,512]{1,2,0:T(8,128)S(1)}, f32[4,128,512]{1,2,0:T(8,128)}, u32[]{:S(2)}) copy-start(f32[4,128,512]{1,2,0:T(8,128)} %copy-done.21) | copy-start | bytes 3145732
  (32 other events, 115.5 us)
Sparse Core Ops, SparseCore 0:
  454.9 106.7 all-gather.5
  570.7 33.6 all-gather.3
